TPU v7x, 128 devices: a whole 4x4x4 slice. The times are simulated.
128 devices in a mesh: dp: 32 (over z, x_lo, y), seq: 4 (over x_hi, core).
Axes of the slice: x: 4 (x_hi: 2, x_lo: 2; x = x_hi * 2 + x_lo), y: 4, z: 4, core: 2. Of those that a mesh axis runs over, the one named last changes fastest.
Arguments:
- queries: bfloat16 [32, 1024, 2560], P('dp', 'seq'), may hold values from -6 to 6
- keys_in: bfloat16 [32, 1024, 2560], P('dp', 'seq'), may hold values from -6 to 6
- values_in: bfloat16 [32, 1024, 2560], P('dp', 'seq'), may hold values from -6 to 6
- head_gain: float32 [20, 128], replicated, may hold values from 0.1 to 1.9
- master_weight: float32 [2560, 5120], P('dp', 'seq'), may hold values from -0.125 to 0.125
- gradient: float32 [2560, 5120], P('dp', 'seq'), may hold values from -6 to 6
- first_moment: float32 [2560, 5120], P('dp', 'seq'), may hold values from -4 to 4
- second_moment: float32 [2560, 5120], P('dp', 'seq'), may hold values from 0.01 to 4
Outputs:
- layer_out: bfloat16 [32, 1024, 5120], P('dp', 'seq')
- new_master: float32 [2560, 5120], P('dp', 'seq')
- new_first: float32 [2560, 5120], P('dp', 'seq')
- new_second: float32 [2560, 5120], P('dp', 'seq')
All inputs are finite; a program needn't handle non-finite values.
Results may differ from a plain program's by a relative error of at most 0.0061.
Values may be sent and summed in bfloat16 or wider, within the bound.
No kernel may reach another device: no remote copies, remote signals or barrier semaphores. Data moves between devices by JAX's collectives and lax.ppermute only.
A program may use at most 192 MiB of HBM per device.

v0:
```python
import math
import jax
import jax.numpy as jnp
from jax import lax
from jax.sharding import PartitionSpec as P

HEAD = 128
H = 20
CH = 128
beta_one = 0.9
beta_two = 0.95
learn_rate = 0.0003
decay_rate = 0.1
adam_eps = 1e-08
step_count = 100
norm_eps = 1e-06


def featurize(block, seq_length):
    positions = jnp.arange(block.shape[0], dtype=jnp.int32).astype(jnp.float32)
    angles = positions * (math.pi / (2.0 * seq_length))
    rectified = jnp.maximum(block.astype(jnp.float32), 0.0)
    cosine = rectified * jnp.cos(angles)[:, None, None]
    sine = rectified * jnp.sin(angles)[:, None, None]
    return jnp.concatenate([cosine, sine], axis=2).astype(jnp.bfloat16)


def block_states(key_feat, value_heads):
    blocks = key_feat.shape[0] // CH
    key_blocks = key_feat.reshape(blocks, CH, key_feat.shape[1], key_feat.shape[2])
    value_blocks = value_heads.reshape(blocks, CH, value_heads.shape[1], value_heads.shape[2])
    return jnp.einsum(
        "cjhf,cjhe->chfe", key_blocks, value_blocks, preferred_element_type=jnp.float32
    )


def attend(query_feat, key_feat, value_heads, states):
    count = query_feat.shape[0]
    heads_here = query_feat.shape[1]
    blocks = count // CH
    query_blocks = query_feat.reshape(blocks, CH, heads_here, 2 * HEAD)
    key_blocks = key_feat.reshape(blocks, CH, heads_here, 2 * HEAD)
    value_blocks = value_heads.reshape(blocks, CH, heads_here, HEAD)
    scores = jnp.einsum(
        "cihf,cjhf->chij", query_blocks, key_blocks, preferred_element_type=jnp.float32
    )
    causal_mask = jnp.arange(CH)[:, None] >= jnp.arange(CH)[None, :]
    scores = jnp.where(causal_mask[None, None], scores, 0.0).astype(jnp.bfloat16)
    inside_block = jnp.einsum(
        "chij,cjhe->cihe", scores, value_blocks, preferred_element_type=jnp.float32
    )
    running = jnp.cumsum(states, axis=0)
    before = jnp.concatenate([jnp.zeros_like(states[:1]), running[:-1]], axis=0)
    before = before.astype(jnp.bfloat16)
    from_before = jnp.einsum(
        "cihf,chfe->cihe", query_blocks, before, preferred_element_type=jnp.float32
    )
    return (inside_block + from_before).reshape(count, heads_here, HEAD)


def normalize(attended, gain_rows):
    mean_square = jnp.mean(attended * attended, axis=2, keepdims=True)
    return (attended * lax.rsqrt(mean_square + norm_eps) * gain_rows[None]).astype(jnp.bfloat16)


def on_device(
    queries, keys_in, values_in, head_gain, master_weight, gradient, first_moment, second_moment
):
    moment_one = beta_one * first_moment + (1.0 - beta_one) * gradient
    moment_two = beta_two * second_moment + (1.0 - beta_two) * gradient * gradient
    corrected = (
        moment_one
        / (1.0 - beta_one**step_count)
        / (jnp.sqrt(moment_two / (1.0 - beta_two**step_count)) + adam_eps)
    )
    updated = master_weight - learn_rate * (corrected + decay_rate * master_weight)
    weights = updated.astype(jnp.bfloat16)
    tokens_here = queries.shape[1]
    seq_length = tokens_here * lax.axis_size("seq")
    query_heads = queries[0].reshape(tokens_here, H, HEAD)
    key_heads = keys_in[0].reshape(tokens_here, H, HEAD)
    value_heads = values_in[0].reshape(tokens_here, H, HEAD)
    query_group, key_group, value_group = (
        lax.all_to_all(query_heads, "seq", split_axis=1, concat_axis=0, tiled=True),
        lax.all_to_all(key_heads, "seq", split_axis=1, concat_axis=0, tiled=True),
        lax.all_to_all(value_heads, "seq", split_axis=1, concat_axis=0, tiled=True),
    )
    heads_here = query_group.shape[1]
    query_feat = featurize(query_group, seq_length)
    key_feat = featurize(key_group, seq_length)
    states = block_states(key_feat, value_group)
    attended = attend(query_feat, key_feat, value_group, states)
    gain_rows = lax.dynamic_slice_in_dim(
        head_gain, lax.axis_index("seq") * heads_here, heads_here, 0
    )
    normed_group = normalize(attended, gain_rows)
    normed_all = lax.all_gather(normed_group, "seq", axis=1, tiled=True)
    normed_all = normed_all.reshape(normed_all.shape[0], H * HEAD)
    cols = lax.all_gather(weights, "dp", axis=0, tiled=True)
    part = jnp.dot(normed_all, cols, preferred_element_type=jnp.float32).astype(jnp.bfloat16)
    projected = lax.all_to_all(part, "seq", split_axis=0, concat_axis=1, tiled=True)
    layer_out = projected[None]
    return (layer_out, updated, moment_one, moment_two)


def solution(mesh):
    in_specs = (
        P("dp", "seq", None),
        P("dp", "seq", None),
        P("dp", "seq", None),
        P(),
        P("dp", "seq"),
        P("dp", "seq"),
        P("dp", "seq"),
        P("dp", "seq"),
    )
    out_specs = (P("dp", "seq", None), P("dp", "seq"), P("dp", "seq"), P("dp", "seq"))
    return jax.shard_map(
        on_device, mesh=mesh, in_specs=in_specs, out_specs=out_specs, check_vma=False
    )
```

profile of v0, /device:TPU:1, one launch (start us, length us, event | category | flops | bytes accessed | tf_op | source)
XLA Modules:
  0.0 368.6 jit_solution(1960539132442733777)
XLA Ops:
  7.2 0.0 copy-start
  7.2 0.0 copy-start.8
  7.2 2.5 copy.30
  9.7 5.8 %all-to-all-start = ((bf16[256,20,128]{0,2,1:T(8,128)(2,1)}), bf16[256,20,128]{0,2,1:T(8,128)(2,1)S(1)}, u32[]{:S(2)}, u32[]{:S(2)}) async-start(bf16[256,20,128]{0,2,1:T(8,128)(2,1)} %bitcast), calls=%async_computation | async-start | bytes 2621440 | tf_op jit(solution)/shard_map/all_to_all | solution.py:84
  15.5 0.0 copy-done.8
  15.5 1.4 copy.35
  17.0 16.5 %all-to-all-done = bf16[256,20,128]{0,2,1:T(8,128)(2,1)S(1)} async-done(((bf16[256,20,128]{0,2,1:T(8,128)(2,1)}), bf16[256,20,128]{0,2,1:T(8,128)(2,1)S(1)}, u32[]{:S(2)}, u32[]{:S(2)}) %all-to-all-start) | async-done | bytes 1310752 | tf_op jit(solution)/shard_map/all_to_all | solution.py:84
  33.4 4.4 %all-to-all-start.1 = ((bf16[256,20,128]{0,2,1:T(8,128)(2,1)}), bf16[256,20,128]{0,2,1:T(8,128)(2,1)S(1)}, u32[]{:S(2)}, u32[]{:S(2)}) async-start(bf16[256,20,128]{0,2,1:T(8,128)(2,1)} %bitcast.5), calls=%async_computation.1 | async-start | bytes 2621440 | tf_op jit(solution)/shard_map/all_to_all | solution.py:85
  37.8 2.4 copy.40
  40.2 0.0 copy-done.6
  40.2 15.5 %all-to-all-done.1 = bf16[256,20,128]{0,2,1:T(8,128)(2,1)S(1)} async-done(((bf16[256,20,128]{0,2,1:T(8,128)(2,1)}), bf16[256,20,128]{0,2,1:T(8,128)(2,1)S(1)}, u32[]{:S(2)}, u32[]{:S(2)}) %all-to-all-start.1) | async-done | bytes 1310752 | tf_op jit(solution)/shard_map/all_to_all | solution.py:85
  55.7 5.1 %all-to-all-start.2 = ((bf16[256,20,128]{0,2,1:T(8,128)(2,1)}), bf16[256,20,128]{0,2,1:T(8,128)(2,1)}, u32[]{:S(2)}, u32[]{:S(2)}) async-start(bf16[256,20,128]{0,2,1:T(8,128)(2,1)} %bitcast.10), calls=%async_computation.2 | async-start | bytes 2621440 | tf_op jit(solution)/shard_map/all_to_all | solution.py:86
  60.9 0.0 all-gather.3.cloned.1.call-start
  60.9 0.0 copy-done
  60.9 0.0 copy-done.7
  60.9 1.6 convert_maximum_fusion.1
  62.5 2.1 copy.32
  64.6 1.6 convert_maximum_fusion
  66.2 2.1 copy.37
  68.3 10.6 %all-to-all-done.2 = bf16[256,20,128]{0,2,1:T(8,128)(2,1)} async-done(((bf16[256,20,128]{0,2,1:T(8,128)(2,1)}), bf16[256,20,128]{0,2,1:T(8,128)(2,1)}, u32[]{:S(2)}, u32[]{:S(2)}) %all-to-all-start.2) | async-done | bytes 1310752 | tf_op jit(solution)/shard_map/all_to_all | solution.py:86
  78.9 2.4 copy.42
  81.3 0.0 copy-done.2
  81.3 3.7 multiply_convert_fusion.1
  85.0 1.1 copy-done.3
  86.1 0.4 copy-done.4
  86.4 0.0 copy-done.5
  86.4 0.9 fusion.6
  87.3 0.6 fusion.23
  87.9 0.2 slice.7
  88.1 5.6 %fusion.7 = f32[8,5,128,128]{3,2,1,0:T(8,128)} fusion(bf16[8,128,5,128]{3,1,2,0:T(8,128)(2,1)} %copy-done.4, bf16[8,128,5,128]{3,1,2,0:T(8,128)(2,1)} %copy-done.3, bf16[8,128,5,128]{3,1,2,0:T(8,128)(2,1)} %get-tuple-element.12, bf16[8,128,5,128]{3,1,2,0:T(8,128)(2,1)} %get-tuple-element.13, pred[128,128]{1,0:T(8,128)(4,1)S(1)} %iota_compare_fusion, ...), kind=kOutput, calls=%fused_computation.19 | convolution fusion | flops 515112960 | bytes 9191424 | tf_op jit(solution)/shard_map/chij,cjhe->cihe/dot_general | solution.py:49
  93.7 3.5 multiply_reduce_fusion
  97.3 0.3 copy.46
  97.6 0.0 copy-start.9
  97.6 0.0 copy-start.10
  97.6 0.0 copy-start.11
  97.6 0.0 copy-start.12
  97.6 1.9 fusion.1
  99.5 0.0 all-gather.3.cloned.1.call-update
  99.5 0.0 all-gather.5.cloned.1.call-start
  99.6 1.3 fusion.21
  100.9 0.0 all-gather.5.cloned.1.call-update
  100.9 43.9 %all-gather.3.cloned.1.call-done = bf16[1024,20,128]{2,0,1:T(8,128)(2,1)} async-done(((bf16[1024,5,128]{2,0,1:T(8,128)(2,1)}), bf16[1024,20,128]{2,0,1:T(8,128)(2,1)}) %all-gather.3.cloned.1.call-update) | async-done | bytes 5242896 | tf_op jit(solution)/shard_map/all_gather | solution.py:97
  144.8 7.9 %copy.47 = bf16[1024,20,128]{0,2,1:T(8,128)(2,1)} copy(bf16[1024,20,128]{2,0,1:T(8,128)(2,1)} %all-gather.3.cloned.1.call-done) | data formatting | bytes 10485760 | tf_op jit(solution)/shard_map/all_gather | solution.py:97
  152.7 136.5 %all-gather.5.cloned.1.call-done = bf16[2560,1280]{1,0:T(8,128)(2,1)} async-done(((bf16[80,1280]{1,0:T(8,128)(2,1)}), bf16[2560,1280]{1,0:T(8,128)(2,1)}) %all-gather.5.cloned.1.call-update) | async-done | bytes 6553616 | tf_op jit(solution)/shard_map/all_gather | solution.py:99
  289.2 10.9 %convolution_convert_fusion = bf16[1024,1280]{1,0:T(8,128)(2,1)S(1)} fusion(bf16[1024,2560]{0,1:T(8,128)(2,1)} %bitcast.40, bf16[2560,1280]{1,0:T(8,128)(2,1)} %all-gather.5.cloned.1.call-done), kind=kOutput, calls=%fused_computation.1 | convolution fusion | flops 6712197120 | bytes 14417920 | tf_op jit(solution)/shard_map/dot_general | solution.py:100
  300.2 56.4 %all_to_all.49 = bf16[4,256,1280]{2,1,0:T(8,128)(2,1)S(1)} all-to-all(bf16[4,256,1280]{2,1,0:T(8,128)(2,1)S(1)} %bitcast.41), channel_id=1, replica_groups=mesh['dp'=32,'seq'=4] {'seq'}, dimensions={0} | all-to-all | bytes 5242880 | tf_op jit(solution)/shard_map/all_to_all | solution.py:101
  356.6 2.0 copy.48
  358.6 3.2 broadcast_in_dim.16
  (16 shorter events, 0.1 us)
Async XLA Ops:
  7.2 53.7 %copy-start = (f32[20,128]{1,0:T(8,128)S(1)}, f32[20,128]{1,0:T(8,128)}, u32[]{:S(2)}) copy-start(f32[20,128]{1,0:T(8,128)} %param.11) | copy-start | bytes 30724
  7.2 8.3 %copy-start.8 = (bf16[1,256,2560]{2,1,0:T(8,128)(2,1)S(1)}, bf16[1,256,2560]{2,1,0:T(8,128)(2,1)}, u32[]{:S(2)}) copy-start(bf16[1,256,2560]{2,1,0:T(8,128)(2,1)} %param.9) | copy-start | bytes 3932164
  9.7 23.7 %all-to-all-start = ((bf16[256,20,128]{0,2,1:T(8,128)(2,1)}), bf16[256,20,128]{0,2,1:T(8,128)(2,1)S(1)}, u32[]{:S(2)}, u32[]{:S(2)}) async-start(bf16[256,20,128]{0,2,1:T(8,128)(2,1)} %bitcast), calls=%async_computation | async-start | bytes 2621440 | tf_op jit(solution)/shard_map/all_to_all | solution.py:84
  33.4 6.8 %copy-start.6 = (bf16[256,20,128]{0,2,1:T(8,128)(2,1)}, bf16[256,20,128]{0,2,1:T(8,128)(2,1)S(1)}, u32[]{:S(2)}) copy-start(bf16[256,20,128]{0,2,1:T(8,128)(2,1)S(1)} %all-to-all-done) | copy-start | bytes 3932164
  33.4 22.3 %all-to-all-start.1 = ((bf16[256,20,128]{0,2,1:T(8,128)(2,1)}), bf16[256,20,128]{0,2,1:T(8,128)(2,1)S(1)}, u32[]{:S(2)}, u32[]{:S(2)}) async-start(bf16[256,20,128]{0,2,1:T(8,128)(2,1)} %bitcast.5), calls=%async_computation.1 | async-start | bytes 2621440 | tf_op jit(solution)/shard_map/all_to_all | solution.py:85
  55.7 5.2 %copy-start.7 = (bf16[256,20,128]{0,2,1:T(8,128)(2,1)}, bf16[256,20,128]{0,2,1:T(8,128)(2,1)S(1)}, u32[]{:S(2)}) copy-start(bf16[256,20,128]{0,2,1:T(8,128)(2,1)S(1)} %all-to-all-done.1) | copy-start | bytes 3932164
  55.7 23.1 %all-to-all-start.2 = ((bf16[256,20,128]{0,2,1:T(8,128)(2,1)}), bf16[256,20,128]{0,2,1:T(8,128)(2,1)}, u32[]{:S(2)}, u32[]{:S(2)}) async-start(bf16[256,20,128]{0,2,1:T(8,128)(2,1)} %bitcast.10), calls=%async_computation.2 | async-start | bytes 2621440 | tf_op jit(solution)/shard_map/all_to_all | solution.py:86
  60.9 83.9 %all-gather.3.cloned.1.call-start = ((), (), s32[]{:S(2)}) async-start(), calls=%async_computation.4 | async-start | bytes 6553600 | tf_op jit(solution)/shard_map/all_gather | solution.py:97
  68.3 13.0 %copy-start.2 = (f32[4,256,5,128]{3,1,0,2:T(8,128)S(1)}, f32[4,256,5,128]{3,1,0,2:T(8,128)}, u32[]{:S(2)}) copy-start(f32[4,256,5,128]{3,1,0,2:T(8,128)} %copy.32) | copy-start | bytes 7864324
  81.3 5.2 %copy-start.5 = (bf16[4,256,5,128]{3,1,0,2:T(8,128)(2,1)S(1)}, bf16[4,256,5,128]{3,1,0,2:T(8,128)(2,1)}, u32[]{:S(2)}) copy-start(bf16[4,256,5,128]{3,1,0,2:T(8,128)(2,1)} %copy.42) | copy-start | bytes 3932164
  85.0 1.1 copy-start.3
  85.0 1.5 copy-start.4
  97.6 2.0 copy-start.9
  97.6 2.0 copy-start.10
  97.6 2.0 copy-start.11
  97.6 2.0 copy-start.12
  99.5 189.7 %all-gather.5.cloned.1.call-start = ((), (), s32[]{:S(2)}) async-start(), calls=%async_computation.5 | async-start | bytes 6758400 | tf_op jit(solution)/shard_map/all_gather | solution.py:99
  356.6 5.2 %copy-start.1 = (f32[20,128]{1,0:T(8,128)S(1)}, f32[20,128]{1,0:T(8,128)}, u32[]{:S(2)}) copy-start(f32[20,128]{1,0:T(8,128)} %param.11) | copy-start | bytes 30724
Sparse Core Ops, SparseCore 0:
  99.6 45.1 all-gather.2
  146.4 142.7 all-gather.4
where the time goes:
time: 369 us
  waiting for transfers between devices  223 us (60%)
  blocking collectives  56.4 us (15%)
  local copies, waits for them, and re-layouts  28 us (8%)
  matrix products  20.9 us (6%)
  starting transfers between devices  15.3 us (4%)
  between operations  14.2 us (4%)
  other arithmetic  10.7 us (3%)
    all_gather x1, waiting for transfers between devices, on_device(): cols = lax.all_gather(weights, 'dp', axis=0, tiled=True)  137 us
    all_to_all x1, blocking collectives, on_device(): lax.all_to_all(part, 'seq', split_axis=0, concat_axis=1, tiled=True)  56.4 us
    all_gather x1, waiting for transfers between devices, on_device(): normed_all = lax.all_gather(normed_group, 'seq', axis=1, tiled=True)  43.9 us
    all_to_all x1, waiting for transfers between devices, on_device(): lax.all_to_all(query_heads, 'seq', split_axis=1, concat_axis=0, tiled=True)  16.5 us
    all_to_all x1, waiting for transfers between devices, on_device(): lax.all_to_all(key_heads, 'seq', split_axis=1, concat_axis=0, tiled=True)  15.5 us
    dot_general x1, matrix products, on_device(): jnp.dot(normed_all, cols, preferred_element_type=jnp.float32)  10.9 us
    all_to_all x1, waiting for transfers between devices, on_device(): lax.all_to_all(value_heads, 'seq', split_axis=1, concat_axis=0, tiled=True)  10.6 us
    all_gather x1, local copies, waits for them, and re-layouts, on_device(): normed_all = lax.all_gather(normed_group, 'seq', axis=1, tiled=True)  7.92 us
  transfers between devices with their start and end apart: 5, of which 5 were waited for; matrix products, arithmetic and copies ran while one was open for 6% of the time, Pallas kernels for 0%

commit v1 on v0

--- a/solution.py
+++ b/solution.py
@@ -96,7 +96,15 @@
     normed_group = normalize(attended, gain_rows)
     normed_all = lax.all_gather(normed_group, "seq", axis=1, tiled=True)
     normed_all = normed_all.reshape(normed_all.shape[0], H * HEAD)
-    cols = lax.all_gather(weights, "dp", axis=0, tiled=True)
+    cols = jnp.concatenate(
+        lax.all_to_all(
+            jnp.stack(lax.psum(1, axis_name="dp") * [weights], 0),
+            axis_name="dp",
+            split_axis=0,
+            concat_axis=0,
+        ),
+        axis=0,
+    )
     part = jnp.dot(normed_all, cols, preferred_element_type=jnp.float32).astype(jnp.bfloat16)
     projected = lax.all_to_all(part, "seq", split_axis=0, concat_axis=1, tiled=True)
     layer_out = projected[None]

time: 369 us -> 289 us (0.78)
  the two profiles are of different devices: /device:TPU:1 before, /device:TPU:48 now
where the time goes in v1:
time: 289 us; the launch traced here: 288 us
  waiting for transfers between devices  152 us (53%)
  blocking collectives  38.5 us (13%)
  local copies, waits for them, and re-layouts  31.3 us (11%)
  matrix products  20.9 us (7%)
  starting transfers between devices  20.4 us (7%)
  between operations  14.2 us (5%)
  other arithmetic  10.6 us (4%)
    all_gather x1, waiting for transfers between devices, on_device(): normed_all = lax.all_gather(normed_group, 'seq', axis=1, tiled=True)  61.8 us
    all_to_all x1, waiting for transfers between devices, on_device(): lax.all_to_all(jnp.stack(lax.psum(1, axis_name='dp') * [weights], 0), axi...  45.2 us
    all_to_all x1, blocking collectives, on_device(): lax.all_to_all(part, 'seq', split_axis=0, concat_axis=1, tiled=True)  38.5 us
    all_to_all x1, waiting for transfers between devices, on_device(): lax.all_to_all(query_heads, 'seq', split_axis=1, concat_axis=0, tiled=True)  17.3 us
    all_to_all x1, waiting for transfers between devices, on_device(): lax.all_to_all(key_heads, 'seq', split_axis=1, concat_axis=0, tiled=True)  16.3 us
    all_to_all x1, waiting for transfers between devices, on_device(): lax.all_to_all(value_heads, 'seq', split_axis=1, concat_axis=0, tiled=True)  11.3 us
    dot_general x1, matrix products, on_device(): jnp.dot(normed_all, cols, preferred_element_type=jnp.float32)  10.9 us
    all_to_all x1, starting transfers between devices, on_device(): lax.all_to_all(jnp.stack(lax.psum(1, axis_name='dp') * [weights], 0), axi...  8.19 us
  transfers between devices with their start and end apart: 5, of which 5 were waited for; matrix products, arithmetic and copies ran while one was open for 8% of the time, Pallas kernels for 0%

profile of v1, /device:TPU:48, one launch (start us, length us, event | category | flops | bytes accessed | tf_op | source)
XLA Modules:
  0.0 287.9 jit_solution(4932504594030135636)
XLA Ops:
  7.2 0.0 copy-start
  7.2 0.0 copy-start.8
  7.2 2.5 copy.30
  9.7 4.3 %all-to-all-start = ((bf16[256,20,128]{0,2,1:T(8,128)(2,1)}), bf16[256,20,128]{0,2,1:T(8,128)(2,1)S(1)}, u32[]{:S(2)}, u32[]{:S(2)}) async-start(bf16[256,20,128]{0,2,1:T(8,128)(2,1)} %bitcast), calls=%async_computation | async-start | bytes 2621440 | tf_op jit(solution)/shard_map/all_to_all | solution.py:84
  14.0 0.0 copy-done.8
  14.0 1.4 copy.35
  15.4 17.3 %all-to-all-done = bf16[256,20,128]{0,2,1:T(8,128)(2,1)S(1)} async-done(((bf16[256,20,128]{0,2,1:T(8,128)(2,1)}), bf16[256,20,128]{0,2,1:T(8,128)(2,1)S(1)}, u32[]{:S(2)}, u32[]{:S(2)}) %all-to-all-start) | async-done | bytes 1310752 | tf_op jit(solution)/shard_map/all_to_all | solution.py:84
  32.8 3.5 %all-to-all-start.1 = ((bf16[256,20,128]{0,2,1:T(8,128)(2,1)}), bf16[256,20,128]{0,2,1:T(8,128)(2,1)S(1)}, u32[]{:S(2)}, u32[]{:S(2)}) async-start(bf16[256,20,128]{0,2,1:T(8,128)(2,1)} %bitcast.5), calls=%async_computation.1 | async-start | bytes 2621440 | tf_op jit(solution)/shard_map/all_to_all | solution.py:85
  36.3 2.4 copy.40
  38.8 0.0 copy-done.6
  38.8 16.3 %all-to-all-done.1 = bf16[256,20,128]{0,2,1:T(8,128)(2,1)S(1)} async-done(((bf16[256,20,128]{0,2,1:T(8,128)(2,1)}), bf16[256,20,128]{0,2,1:T(8,128)(2,1)S(1)}, u32[]{:S(2)}, u32[]{:S(2)}) %all-to-all-start.1) | async-done | bytes 1310752 | tf_op jit(solution)/shard_map/all_to_all | solution.py:85
  55.1 4.3 %all-to-all-start.2 = ((bf16[256,20,128]{0,2,1:T(8,128)(2,1)}), bf16[256,20,128]{0,2,1:T(8,128)(2,1)}, u32[]{:S(2)}, u32[]{:S(2)}) async-start(bf16[256,20,128]{0,2,1:T(8,128)(2,1)} %bitcast.10), calls=%async_computation.2 | async-start | bytes 2621440 | tf_op jit(solution)/shard_map/all_to_all | solution.py:86
  59.4 0.0 all-gather.2.cloned.1.call-start
  59.5 1.6 convert_maximum_fusion.1
  61.1 2.1 copy.32
  63.2 1.6 convert_maximum_fusion
  64.8 2.1 copy.37
  66.9 11.3 %all-to-all-done.2 = bf16[256,20,128]{0,2,1:T(8,128)(2,1)} async-done(((bf16[256,20,128]{0,2,1:T(8,128)(2,1)}), bf16[256,20,128]{0,2,1:T(8,128)(2,1)}, u32[]{:S(2)}, u32[]{:S(2)}) %all-to-all-start.2) | async-done | bytes 1310752 | tf_op jit(solution)/shard_map/all_to_all | solution.py:86
  78.2 2.4 copy.42
  80.6 3.7 %multiply_convert_fusion.1 = (bf16[8,128,5,128]{3,1,2,0:T(8,128)(2,1)S(1)}, bf16[8,128,5,128]{3,1,2,0:T(8,128)(2,1)S(1)}, bf16[8,128,5,128]{3,1,2,0:T(8,128)(2,1)}, bf16[8,128,5,128]{3,1,2,0:T(8,128)(2,1)}) fusion(f32[8,128,5,128]{3,1,0,2:T(8,128)} %bitcast.38, f32[8,128]{1,0:T(8,128)S(1)} %get-tuple-element.17, f32[8,128]{1,0:T(8,128)S(1)} %get-tuple-element.16, ...), kind=kLoop, calls=%fused_computation.13 | loop fusion | flops 5242880 | bytes 10493952 | tf_op jit(solution)/shard_map/convert.3
  84.3 1.1 copy-done.3
  85.4 0.4 copy-done.4
  85.8 0.9 fusion.6
  86.7 0.6 fusion.23
  87.3 0.2 slice.7
  87.5 5.6 %fusion.7 = f32[8,5,128,128]{3,2,1,0:T(8,128)} fusion(bf16[8,128,5,128]{3,1,2,0:T(8,128)(2,1)} %copy-done.4, bf16[8,128,5,128]{3,1,2,0:T(8,128)(2,1)} %copy-done.3, bf16[8,128,5,128]{3,1,2,0:T(8,128)(2,1)} %get-tuple-element.12, bf16[8,128,5,128]{3,1,2,0:T(8,128)(2,1)} %get-tuple-element.13, pred[128,128]{1,0:T(8,128)(4,1)S(1)} %iota_compare_fusion, ...), kind=kOutput, calls=%fused_computation.19 | convolution fusion | flops 515112960 | bytes 9191424 | tf_op jit(solution)/shard_map/chij,cjhe->cihe/dot_general | solution.py:49
  93.1 3.5 %multiply_reduce_fusion = (f32[8,128,5]{1,2,0:T(8,128)S(1)}, f32[8,128,5,128]{3,1,2,0:T(8,128)S(1)}) fusion(bf16[7,5,256,128]{3,2,1,0:T(8,128)(2,1)S(1)} %slice.7, bf16[8,128,5,128]{3,1,2,0:T(8,128)(2,1)} %get-tuple-element.12, bf16[8,128,5,128]{3,1,2,0:T(8,128)(2,1)} %get-tuple-element.13, f32[8,5,128,128]{3,2,1,0:T(8,128)} %fusion.7), kind=kOutput, calls=%fused_computation.8 | convolution fusion | flops 342748160 | bytes 10178560 | tf_op jit(solution)/shard_map/cihf,chfe->cihe/dot_general | solution.py:55
  96.6 0.3 copy.46
  96.9 0.0 copy-start.9
  96.9 0.0 copy-start.10
  97.0 0.0 copy-start.11
  97.0 0.0 copy-start.12
  97.0 1.9 fusion.1
  98.8 0.0 all-gather.2.cloned.1.call-update
  98.9 0.0 copy-done.9
  98.9 0.0 copy-done.10
  98.9 0.0 copy-done.11
  98.9 0.0 copy-done.12
  98.9 1.2 fusion.21
  100.1 3.2 %stack.2 = bf16[32,80,1280]{2,1,0:T(8,128)(2,1)} broadcast(bf16[80,1280]{1,0:T(8,128)(2,1)S(1)} %get-tuple-element.4), dimensions={1,2} | broadcast | bytes 6758400 | tf_op jit(solution)/shard_map/stack | solution.py:101
  103.3 8.2 %all-to-all-start.3 = ((bf16[32,80,1280]{2,1,0:T(8,128)(2,1)}), bf16[32,80,1280]{2,1,0:T(8,128)(2,1)}, u32[]{:S(2)}, u32[]{:S(2)}) async-start(bf16[32,80,1280]{2,1,0:T(8,128)(2,1)} %stack.2), calls=%async_computation.3 | async-start | bytes 13107200 | tf_op jit(solution)/shard_map/all_to_all | solution.py:100
  111.5 61.8 %all-gather.2.cloned.1.call-done = bf16[1024,20,128]{2,0,1:T(8,128)(2,1)} async-done(((bf16[1024,5,128]{2,0,1:T(8,128)(2,1)}), bf16[1024,20,128]{2,0,1:T(8,128)(2,1)}) %all-gather.2.cloned.1.call-update) | async-done | bytes 5242896 | tf_op jit(solution)/shard_map/all_gather | solution.py:97
  173.4 7.9 %copy.47 = bf16[1024,20,128]{0,2,1:T(8,128)(2,1)} copy(bf16[1024,20,128]{2,0,1:T(8,128)(2,1)} %all-gather.2.cloned.1.call-done) | data formatting | bytes 10485760 | tf_op jit(solution)/shard_map/all_gather | solution.py:97
  181.3 45.2 %all-to-all-done.3 = bf16[32,80,1280]{2,1,0:T(8,128)(2,1)} async-done(((bf16[32,80,1280]{2,1,0:T(8,128)(2,1)}), bf16[32,80,1280]{2,1,0:T(8,128)(2,1)}, u32[]{:S(2)}, u32[]{:S(2)}) %all-to-all-start.3) | async-done | bytes 6553632 | tf_op jit(solution)/shard_map/all_to_all | solution.py:100
  226.5 10.9 %convolution_convert_fusion = bf16[1024,1280]{1,0:T(8,128)(2,1)S(1)} fusion(bf16[1024,2560]{0,1:T(8,128)(2,1)} %bitcast.41, bf16[2560,1280]{1,0:T(8,128)(2,1)} %bitcast.20), kind=kOutput, calls=%fused_computation.1 | convolution fusion | flops 6712197120 | bytes 14417920 | tf_op jit(solution)/shard_map/dot_general | solution.py:108
  237.4 38.5 %all_to_all.54 = bf16[4,256,1280]{2,1,0:T(8,128)(2,1)S(1)} all-to-all(bf16[4,256,1280]{2,1,0:T(8,128)(2,1)S(1)} %bitcast.42), channel_id=1, replica_groups=mesh['dp'=32,'seq'=4] {'seq'}, dimensions={0} | all-to-all | bytes 5242880 | tf_op jit(solution)/shard_map/all_to_all | solution.py:109
  275.8 2.0 copy.48
  277.9 3.2 %broadcast_in_dim.16 = bf16[1,256,5120]{2,1,0:T(8,128)(2,1)} reshape(bf16[256,4,1280]{2,1,0:T(4,128)(2,1)S(1)} %copy.48) | data formatting | bytes 5242880 | tf_op jit(solution)/shard_map/broadcast_in_dim | solution.py:110
  (16 shorter events, 0.1 us)
Async XLA Ops:
  7.2 52.3 %copy-start = (f32[20,128]{1,0:T(8,128)S(1)}, f32[20,128]{1,0:T(8,128)}, u32[]{:S(2)}) copy-start(f32[20,128]{1,0:T(8,128)} %param.11) | copy-start | bytes 30724
  7.2 6.8 %copy-start.8 = (bf16[1,256,2560]{2,1,0:T(8,128)(2,1)S(1)}, bf16[1,256,2560]{2,1,0:T(8,128)(2,1)}, u32[]{:S(2)}) copy-start(bf16[1,256,2560]{2,1,0:T(8,128)(2,1)} %param.9) | copy-start | bytes 3932164
  9.7 23.1 %all-to-all-start = ((bf16[256,20,128]{0,2,1:T(8,128)(2,1)}), bf16[256,20,128]{0,2,1:T(8,128)(2,1)S(1)}, u32[]{:S(2)}, u32[]{:S(2)}) async-start(bf16[256,20,128]{0,2,1:T(8,128)(2,1)} %bitcast), calls=%async_computation | async-start | bytes 2621440 | tf_op jit(solution)/shard_map/all_to_all | solution.py:84
  32.8 6.0 %copy-start.6 = (bf16[256,20,128]{0,2,1:T(8,128)(2,1)}, bf16[256,20,128]{0,2,1:T(8,128)(2,1)S(1)}, u32[]{:S(2)}) copy-start(bf16[256,20,128]{0,2,1:T(8,128)(2,1)S(1)} %all-to-all-done) | copy-start | bytes 3932164
  32.8 22.3 %all-to-all-start.1 = ((bf16[256,20,128]{0,2,1:T(8,128)(2,1)}), bf16[256,20,128]{0,2,1:T(8,128)(2,1)S(1)}, u32[]{:S(2)}, u32[]{:S(2)}) async-start(bf16[256,20,128]{0,2,1:T(8,128)(2,1)} %bitcast.5), calls=%async_computation.1 | async-start | bytes 2621440 | tf_op jit(solution)/shard_map/all_to_all | solution.py:85
  55.1 4.4 %copy-start.7 = (bf16[256,20,128]{0,2,1:T(8,128)(2,1)}, bf16[256,20,128]{0,2,1:T(8,128)(2,1)S(1)}, u32[]{:S(2)}) copy-start(bf16[256,20,128]{0,2,1:T(8,128)(2,1)S(1)} %all-to-all-done.1) | copy-start | bytes 3932164
  55.1 23.1 %all-to-all-start.2 = ((bf16[256,20,128]{0,2,1:T(8,128)(2,1)}), bf16[256,20,128]{0,2,1:T(8,128)(2,1)}, u32[]{:S(2)}, u32[]{:S(2)}) async-start(bf16[256,20,128]{0,2,1:T(8,128)(2,1)} %bitcast.10), calls=%async_computation.2 | async-start | bytes 2621440 | tf_op jit(solution)/shard_map/all_to_all | solution.py:86
  59.4 114.0 %all-gather.2.cloned.1.call-start = ((), (), s32[]{:S(2)}) async-start(), calls=%async_computation.5 | async-start | bytes 6553600 | tf_op jit(solution)/shard_map/all_gather | solution.py:97
  66.9 13.8 %copy-start.2 = (f32[4,256,5,128]{3,1,0,2:T(8,128)S(1)}, f32[4,256,5,128]{3,1,0,2:T(8,128)}, u32[]{:S(2)}) copy-start(f32[4,256,5,128]{3,1,0,2:T(8,128)} %copy.32) | copy-start | bytes 7864324
  80.6 5.2 %copy-start.5 = (bf16[4,256,5,128]{3,1,0,2:T(8,128)(2,1)S(1)}, bf16[4,256,5,128]{3,1,0,2:T(8,128)(2,1)}, u32[]{:S(2)}) copy-start(bf16[4,256,5,128]{3,1,0,2:T(8,128)(2,1)} %copy.42) | copy-start | bytes 3932164
  84.3 1.1 copy-start.3
  84.3 1.5 copy-start.4
  96.9 1.9 copy-start.9
  96.9 1.9 copy-start.10
  97.0 1.9 copy-start.11
  97.0 1.9 copy-start.12
  103.3 123.1 %all-to-all-start.3 = ((bf16[32,80,1280]{2,1,0:T(8,128)(2,1)}), bf16[32,80,1280]{2,1,0:T(8,128)(2,1)}, u32[]{:S(2)}, u32[]{:S(2)}) async-start(bf16[32,80,1280]{2,1,0:T(8,128)(2,1)} %stack.2), calls=%async_computation.3 | async-start | bytes 13107200 | tf_op jit(solution)/shard_map/all_to_all | solution.py:100
  275.8 5.2 %copy-start.1 = (f32[20,128]{1,0:T(8,128)S(1)}, f32[20,128]{1,0:T(8,128)}, u32[]{:S(2)}) copy-start(f32[20,128]{1,0:T(8,128)} %param.11) | copy-start | bytes 30724
Sparse Core Ops, SparseCore 0:
  99.0 74.3 all-gather.1
